TPU v7x, 32 devices: a whole 2x2x4 slice. The times are simulated.
32 devices in a mesh: parts: 2 (over y), ctx: 8 (over z, x), tp: 2 (over core).
Axes of the slice: x: 2, y: 2, z: 4, core: 2. Of those that a mesh axis runs over, the one named last changes fastest.
Arguments:
- queries: bfloat16 [2048, 8192], P(('parts', 'ctx'), 'tp'), parts along dimension 0, may hold values from -9 to 9
- episode_key_cache: bfloat16 [128, 16, 1024], P(None, ('parts', 'ctx'), 'tp'), parts along dimension 1, may hold values from -9 to 9
- episode_value_cache: bfloat16 [128, 16, 1024], P(None, ('parts', 'ctx'), 'tp'), parts along dimension 1, may hold values from -6 to 6
- output_gradient: bfloat16 [2048, 8192], P(('parts', 'ctx'), 'tp'), parts along dimension 0, may hold values from -6 to 6
- block_lists: int32 [16, 2], P(('parts', 'ctx')), parts along dimension 0, may hold values from 0 to 7, as said below
- block_counts: int32 [16], P(('parts', 'ctx')), parts along dimension 0, may hold values from 1 to 2
Outputs:
- attn_out: bfloat16 [2048, 8192], P(('parts', 'ctx'), 'tp'), parts along dimension 0
- query_grad: bfloat16 [2048, 8192], P(('parts', 'ctx'), 'tp'), parts along dimension 0
- key_cache_gradient: bfloat16 [128, 16, 1024], P(None, ('parts', 'ctx'), 'tp'), parts along dimension 1
- value_cache_gradient: bfloat16 [128, 16, 1024], P(None, ('parts', 'ctx'), 'tp'), parts along dimension 1
There are 2 independent parts, one for each index of `parts`. A program takes and returns all parts, laid end to end along the dimension named above; each array names one. Nothing has to cross between parts.
Inputs may be any that keep to these rules, and one draw needn't show every extreme that they name: `block_lists`: each row names 2 different key blocks; a query block reads only its first block_counts entries.
All inputs are finite; a program needn't handle non-finite values.
Results may differ from a plain program's by a relative error of at most 0.0085.
The roundings to bfloat16 on the way count: a program that leaves them out, or rounds other values in their place, can miss the bound.
Values may be sent and summed in bfloat16 or wider, within the bound.
No kernel may reach another device: no remote copies, remote signals or barrier semaphores. Data moves between devices by JAX's collectives and lax.ppermute only.
A program may use at most 64 MiB of HBM per device.

v0:
```python
import jax
import jax.numpy as jnp
from jax import lax
from jax.sharding import PartitionSpec as P

QUERY_HEADS = 64
KEY_VALUE_HEADS = 8
HEAD_SIZE = 128
LIST = 2


def attend_group(query_part, key_part, value_part, grad_part, live_slots):
    score_scale = HEAD_SIZE ** (-0.5)
    scores = score_scale * jnp.einsum(
        "qah,jkh->aqjk", query_part, key_part, preferred_element_type=jnp.float32
    )
    masked = jnp.where(live_slots[None, None, :, None], scores, -jnp.inf)
    row_peak = jnp.max(masked, axis=(2, 3), keepdims=True)
    exponent = jnp.exp(masked - row_peak)
    weights = exponent / jnp.sum(exponent, axis=(2, 3), keepdims=True)
    weights_low = weights.astype(jnp.bfloat16)
    attended = jnp.einsum(
        "aqjk,jkh->qah", weights_low, value_part, preferred_element_type=jnp.float32
    ).astype(jnp.bfloat16)
    attended = lax.optimization_barrier(attended)
    row_delta = jnp.sum(grad_part.astype(jnp.float32) * attended.astype(jnp.float32), axis=2)
    weight_grad = jnp.einsum(
        "qah,jkh->aqjk", grad_part, value_part, preferred_element_type=jnp.float32
    )
    score_grad = (weights * (weight_grad - row_delta.T[:, :, None, None])).astype(jnp.bfloat16)
    query_grad = (
        score_scale
        * jnp.einsum("aqjk,jkh->qah", score_grad, key_part, preferred_element_type=jnp.float32)
    ).astype(jnp.bfloat16)
    key_piece = score_scale * jnp.einsum(
        "aqjk,qah->jkh", score_grad, query_part, preferred_element_type=jnp.float32
    )
    value_piece = jnp.einsum(
        "aqjk,qah->jkh", weights_low, grad_part, preferred_element_type=jnp.float32
    )
    return (attended, query_grad, key_piece, value_piece)


def arrange_rows(arrived):
    row_count, slot_count, peer_count, column_count = arrived.shape
    return jnp.transpose(arrived, (1, 2, 0, 3)).reshape(
        slot_count, peer_count * row_count, column_count
    )


def split_rows(pieces, row_count):
    slot_count, row_total, column_count = pieces.shape
    shaped = pieces.reshape(slot_count, row_total // row_count, row_count, column_count)
    return jnp.transpose(shaped, (2, 0, 1, 3))


def owner_sum(arrived, selector):
    summed = jnp.einsum("rjpc,jpn->rnc", arrived, selector, precision=lax.Precision.HIGHEST)
    return summed.astype(jnp.bfloat16)


def shards(
    queries, episode_key_cache, episode_value_cache, output_gradient, block_lists, block_counts
):
    held_keys, held_values = (
        lax.all_to_all(episode_key_cache, "ctx", split_axis=0, concat_axis=1, tiled=True),
        lax.all_to_all(episode_value_cache, "ctx", split_axis=0, concat_axis=1, tiled=True),
    )
    row_count = held_keys.shape[0]
    block_total = held_keys.shape[1]
    local_groups = held_keys.shape[2] // HEAD_SIZE
    queries_per_group = QUERY_HEADS // KEY_VALUE_HEADS
    query_rows = queries.shape[0]
    listed_all = lax.all_gather(block_lists, "ctx", axis=0, tiled=True)
    wanted = listed_all.T
    live_slots = jnp.arange(LIST, dtype=jnp.int32) < block_counts[0]
    selector = (
        wanted[:, :, None] == jnp.arange(block_total, dtype=jnp.int32)[None, None, :]
    ).astype(jnp.float32)
    picked_keys = jnp.take(held_keys, wanted, axis=1)
    picked_values = jnp.take(held_values, wanted, axis=1)

    def run_group(group_index, key_rows, value_rows):
        first_col = group_index * queries_per_group * HEAD_SIZE
        last_col = first_col + queries_per_group * HEAD_SIZE
        query_part = queries[:, first_col:last_col].reshape(
            query_rows, queries_per_group, HEAD_SIZE
        )
        grad_part = output_gradient[:, first_col:last_col].reshape(
            query_rows, queries_per_group, HEAD_SIZE
        )
        return attend_group(query_part, key_rows, value_rows, grad_part, live_slots)

    arrived_keys, arrived_values = (
        lax.all_to_all(picked_keys, "ctx", split_axis=2, concat_axis=2, tiled=True),
        lax.all_to_all(picked_values, "ctx", split_axis=2, concat_axis=2, tiled=True),
    )
    fetched_keys = arrange_rows(arrived_keys)
    fetched_values = arrange_rows(arrived_values)
    results = [
        run_group(
            group_index,
            fetched_keys[:, :, group_index * HEAD_SIZE : (group_index + 1) * HEAD_SIZE],
            fetched_values[:, :, group_index * HEAD_SIZE : (group_index + 1) * HEAD_SIZE],
        )
        for group_index in range(local_groups)
    ]
    key_pieces = jnp.concatenate([outcome[2] for outcome in results], axis=2)
    value_pieces = jnp.concatenate([outcome[3] for outcome in results], axis=2)
    back_keys, back_values = (
        lax.all_to_all(
            split_rows(key_pieces, row_count).astype(jnp.bfloat16),
            "ctx",
            split_axis=2,
            concat_axis=2,
            tiled=True,
        ).astype(jnp.float32),
        lax.all_to_all(
            split_rows(value_pieces, row_count).astype(jnp.bfloat16),
            "ctx",
            split_axis=2,
            concat_axis=2,
            tiled=True,
        ).astype(jnp.float32),
    )
    row_key_grad = owner_sum(back_keys, selector)
    row_value_grad = owner_sum(back_values, selector)
    key_cache_gradient, value_cache_gradient = (
        lax.all_to_all(row_key_grad, "ctx", split_axis=1, concat_axis=0, tiled=True),
        lax.all_to_all(row_value_grad, "ctx", split_axis=1, concat_axis=0, tiled=True),
    )
    attn_out = jnp.concatenate(
        [outcome[0].reshape(query_rows, queries_per_group * HEAD_SIZE) for outcome in results],
        axis=1,
    )
    query_grad = jnp.concatenate(
        [outcome[1].reshape(query_rows, queries_per_group * HEAD_SIZE) for outcome in results],
        axis=1,
    )
    return (attn_out, query_grad, key_cache_gradient, value_cache_gradient)


def solution(mesh):
    placed = (
        P(("parts", "ctx"), "tp"),
        P(None, ("parts", "ctx"), "tp"),
        P(None, ("parts", "ctx"), "tp"),
        P(("parts", "ctx"), "tp"),
        P(("parts", "ctx"), None),
        P(("parts", "ctx")),
    )
    return jax.shard_map(
        shards,
        mesh=mesh,
        in_specs=placed,
        out_specs=(
            P(("parts", "ctx"), "tp"),
            P(("parts", "ctx"), "tp"),
            P(None, ("parts", "ctx"), "tp"),
            P(None, ("parts", "ctx"), "tp"),
        ),
        check_vma=False,
    )
```

profile of v0, /device:TPU:0, one launch (start us, length us, event | category | flops | bytes accessed | tf_op | source)
XLA Modules:
  0.0 133.8 jit_solution(3935929716690283083)
XLA Ops:
  1.1 1.6 %reduce = bf16[128,512]{1,0:T(8,128)(2,1)S(1)} reduce(bf16[128,1,512]{2,0,1:T(8,128)(2,1)} %param.10, bf16[]{:T(256)} %broadcast.110), dimensions={1}, to_apply=%copy.184.reduce_sub_computation | reduce | bytes 262146 | tf_op args[2]
  3.5 7.3 %all-to-all-start = ((bf16[8,2,4096]{2,1,0:T(2,128)(2,1)}), bf16[8,2,4096]{2,1,0:T(2,128)(2,1)S(1)}, u32[]{:S(2)}, u32[]{:S(2)}) async-start(bf16[8,2,4096]{2,1,0:T(2,128)(2,1)} %reshape.189), calls=%async_computation | async-start | bytes 262144 | tf_op jit(solution)/shard_map/all_to_all | solution.py:67
  10.7 21.1 %all-gather = s32[8,1,2]{2,1,0:T(1,128)S(1)} all-gather(s32[1,1,2]{2,1,0:T(1,128)} %bitcast.467), channel_id=1, replica_groups=mesh['parts'=2,'ctx'=8,'tp'=2] {'ctx'}, dimensions={0}, use_global_device_ids=true | all-gather | bytes 72 | tf_op jit(solution)/shard_map/all_gather | solution.py:74
  32.1 1.6 %reduce.1 = bf16[128,512]{1,0:T(8,128)(2,1)S(1)} reduce(bf16[128,1,512]{2,0,1:T(8,128)(2,1)} %param.9, bf16[]{:T(256)} %broadcast.110), dimensions={1}, to_apply=%copy.188.reduce_sub_computation | reduce | bytes 262146 | tf_op args[1]
  34.4 3.4 %all-to-all-start.2 = ((bf16[8,2,4096]{2,1,0:T(2,128)(2,1)}), bf16[8,2,4096]{2,1,0:T(2,128)(2,1)S(1)}, u32[]{:S(2)}, u32[]{:S(2)}) async-start(bf16[8,2,4096]{2,1,0:T(2,128)(2,1)} %reshape.187), calls=%async_computation.2 | async-start | bytes 262144 | tf_op jit(solution)/shard_map/all_to_all | solution.py:66
  37.9 7.1 %all-to-all-done.2 = bf16[8,2,4096]{2,1,0:T(2,128)(2,1)S(1)} async-done(((bf16[8,2,4096]{2,1,0:T(2,128)(2,1)}), bf16[8,2,4096]{2,1,0:T(2,128)(2,1)S(1)}, u32[]{:S(2)}, u32[]{:S(2)}) %all-to-all-start.2) | async-done | bytes 131104 | tf_op jit(solution)/shard_map/all_to_all | solution.py:66
  47.2 3.4 %all-to-all-start.3 = ((bf16[16,2,8,512]{3,0,1,2:T(8,128)(2,1)}), bf16[16,2,8,512]{3,0,1,2:T(8,128)(2,1)S(1)}, u32[]{:S(2)}, u32[]{:S(2)}) async-start(bf16[16,2,8,512]{3,0,1,2:T(8,128)(2,1)} %copy.189), calls=%async_computation.3 | async-start | bytes 524288 | tf_op jit(solution)/shard_map/all_to_all | solution.py:95
  52.6 0.9 fusion.71
  53.5 1.2 copy.210
  56.6 2.2 %all-to-all-done.3 = bf16[16,2,8,512]{3,0,1,2:T(8,128)(2,1)S(1)} async-done(((bf16[16,2,8,512]{3,0,1,2:T(8,128)(2,1)}), bf16[16,2,8,512]{3,0,1,2:T(8,128)(2,1)S(1)}, u32[]{:S(2)}, u32[]{:S(2)}) %all-to-all-start.3) | async-done | bytes 262176 | tf_op jit(solution)/shard_map/all_to_all | solution.py:95
  58.8 4.0 %all-to-all-start.1 = ((bf16[16,2,8,512]{3,0,1,2:T(8,128)(2,1)}), bf16[16,2,8,512]{3,0,1,2:T(8,128)(2,1)}, u32[]{:S(2)}, u32[]{:S(2)}) async-start(bf16[16,2,8,512]{3,0,1,2:T(8,128)(2,1)} %copy.185), calls=%async_computation.1 | async-start | bytes 524288 | tf_op jit(solution)/shard_map/all_to_all | solution.py:96
  64.2 6.8 %all-to-all-done.1 = bf16[16,2,8,512]{3,0,1,2:T(8,128)(2,1)} async-done(((bf16[16,2,8,512]{3,0,1,2:T(8,128)(2,1)}), bf16[16,2,8,512]{3,0,1,2:T(8,128)(2,1)}, u32[]{:S(2)}, u32[]{:S(2)}) %all-to-all-start.1) | async-done | bytes 262176 | tf_op jit(solution)/shard_map/all_to_all | solution.py:96
  71.1 1.0 copy.186
  73.4 1.0 fusion.28
  76.8 0.9 fusion.30
  78.7 0.9 fusion.50
  83.1 2.0 %copy.239 = bf16[16,2,8,512]{3,1,0,2:T(2,128)(2,1)} copy(bf16[16,2,8,512]{3,0,2,1:T(8,128)(2,1)} %bitcast.447) | data formatting | bytes 524288 | tf_op jit(solution)/shard_map/convert_element_type | solution.py:112
  85.0 4.0 %all-to-all-start.4 = ((bf16[16,2,8,512]{3,1,0,2:T(2,128)(2,1)}), bf16[16,2,8,512]{3,1,0,2:T(2,128)(2,1)}, u32[]{:S(2)}, u32[]{:S(2)}) async-start(bf16[16,2,8,512]{3,1,0,2:T(2,128)(2,1)} %copy.239), calls=%async_computation.4 | async-start | bytes 524288 | tf_op jit(solution)/shard_map/all_to_all | solution.py:111
  89.1 1.0 fusion.29
  90.4 1.1 copy.231
  91.6 1.1 copy.232
  93.9 0.9 pad_maximum_fusion.3
  94.9 1.0 copy.247
  95.9 1.5 %all-to-all-done.4 = bf16[16,2,8,512]{3,1,0,2:T(2,128)(2,1)} async-done(((bf16[16,2,8,512]{3,1,0,2:T(2,128)(2,1)}), bf16[16,2,8,512]{3,1,0,2:T(2,128)(2,1)}, u32[]{:S(2)}, u32[]{:S(2)}) %all-to-all-start.4) | async-done | bytes 262176 | tf_op jit(solution)/shard_map/all_to_all | solution.py:111
  97.3 4.4 %all-to-all-start.6 = ((bf16[16,2,8,512]{3,1,0,2:T(2,128)(2,1)}), bf16[16,2,8,512]{3,1,0,2:T(2,128)(2,1)S(1)}, u32[]{:S(2)}, u32[]{:S(2)}) async-start(bf16[16,2,8,512]{3,1,0,2:T(2,128)(2,1)} %copy.247), calls=%async_computation.6 | async-start | bytes 524288 | tf_op jit(solution)/shard_map/all_to_all | solution.py:118
  102.3 1.2 fusion.39
  104.3 6.1 %all-to-all-done.6 = bf16[16,2,8,512]{3,1,0,2:T(2,128)(2,1)S(1)} async-done(((bf16[16,2,8,512]{3,1,0,2:T(2,128)(2,1)}), bf16[16,2,8,512]{3,1,0,2:T(2,128)(2,1)S(1)}, u32[]{:S(2)}, u32[]{:S(2)}) %all-to-all-start.6) | async-done | bytes 262176 | tf_op jit(solution)/shard_map/all_to_all | solution.py:118
  110.4 3.8 %all-to-all-start.5 = ((bf16[16,8,512]{2,0,1:T(8,128)(2,1)}), bf16[16,8,512]{2,0,1:T(8,128)(2,1)S(1)}, u32[]{:S(2)}, u32[]{:S(2)}) async-start(bf16[16,8,512]{2,0,1:T(8,128)(2,1)} %copy.241), calls=%async_computation.5 | async-start | bytes 262144 | tf_op jit(solution)/shard_map/all_to_all | solution.py:129
  115.2 6.5 %all-to-all-done.5 = bf16[16,8,512]{2,0,1:T(8,128)(2,1)S(1)} async-done(((bf16[16,8,512]{2,0,1:T(8,128)(2,1)}), bf16[16,8,512]{2,0,1:T(8,128)(2,1)S(1)}, u32[]{:S(2)}, u32[]{:S(2)}) %all-to-all-start.5) | async-done | bytes 131104 | tf_op jit(solution)/shard_map/all_to_all | solution.py:129
  121.8 3.4 %all-to-all-start.7 = ((bf16[16,8,512]{2,0,1:T(8,128)(2,1)}), bf16[16,8,512]{2,0,1:T(8,128)(2,1)S(1)}, u32[]{:S(2)}, u32[]{:S(2)}) async-start(bf16[16,8,512]{2,0,1:T(8,128)(2,1)} %copy.249), calls=%async_computation.7 | async-start | bytes 262144 | tf_op jit(solution)/shard_map/all_to_all | solution.py:130
  125.2 1.5 %pad_maximum_fusion = (bf16[128,4096]{1,0:T(8,128)(2,1)}, bf16[128,4096]{1,0:T(8,128)(2,1)}) fusion(bf16[128,1024]{1,0:T(8,128)(2,1)S(1)} %copy.209, bf16[128,1024]{1,0:T(8,128)(2,1)S(1)} %copy-done.7, bf16[128,1024]{1,0:T(8,128)(2,1)S(1)} %copy.207, bf16[128,1024]{1,0:T(8,128)(2,1)S(1)} %copy.206, bf16[128,1024]{1,0:T(8,128)(2,1)S(1)} %copy.233, ...), kind=kLoop, calls=%fused_computation.80 | loop fusion | flops 8388608 | bytes 4194304 | tf_op jit(solution)/shard_map/concatenate | solution.py:132
  126.7 5.8 %all-to-all-done.7 = bf16[16,8,512]{2,0,1:T(8,128)(2,1)S(1)} async-done(((bf16[16,8,512]{2,0,1:T(8,128)(2,1)}), bf16[16,8,512]{2,0,1:T(8,128)(2,1)S(1)}, u32[]{:S(2)}, u32[]{:S(2)}) %all-to-all-start.7) | async-done | bytes 131104 | tf_op jit(solution)/shard_map/all_to_all | solution.py:130
  (98 shorter events, 22.1 us)
Async XLA Ops:
  3.5 30.9 %all-to-all-start = ((bf16[8,2,4096]{2,1,0:T(2,128)(2,1)}), bf16[8,2,4096]{2,1,0:T(2,128)(2,1)S(1)}, u32[]{:S(2)}, u32[]{:S(2)}) async-start(bf16[8,2,4096]{2,1,0:T(2,128)(2,1)} %reshape.189), calls=%async_computation | async-start | bytes 262144 | tf_op jit(solution)/shard_map/all_to_all | solution.py:67
  34.4 10.7 %all-to-all-start.2 = ((bf16[8,2,4096]{2,1,0:T(2,128)(2,1)}), bf16[8,2,4096]{2,1,0:T(2,128)(2,1)S(1)}, u32[]{:S(2)}, u32[]{:S(2)}) async-start(bf16[8,2,4096]{2,1,0:T(2,128)(2,1)} %reshape.187), calls=%async_computation.2 | async-start | bytes 262144 | tf_op jit(solution)/shard_map/all_to_all | solution.py:66
  46.3 4.3 %copy-start.8 = (bf16[128,4096]{1,0:T(8,128)(2,1)S(1)}, bf16[128,4096]{1,0:T(8,128)(2,1)}, u32[]{:S(2)}) copy-start(bf16[128,4096]{1,0:T(8,128)(2,1)} %param.8) | copy-start | bytes 3145732
  47.2 11.6 %all-to-all-start.3 = ((bf16[16,2,8,512]{3,0,1,2:T(8,128)(2,1)}), bf16[16,2,8,512]{3,0,1,2:T(8,128)(2,1)S(1)}, u32[]{:S(2)}, u32[]{:S(2)}) async-start(bf16[16,2,8,512]{3,0,1,2:T(8,128)(2,1)} %copy.189), calls=%async_computation.3 | async-start | bytes 524288 | tf_op jit(solution)/shard_map/all_to_all | solution.py:95
  51.4 1.2 copy-start.9
  53.5 2.2 %copy-start.11 = (bf16[128,1024]{1,0:T(8,128)(2,1)S(1)}, bf16[128,1024]{1,0:T(8,128)(2,1)}, u32[]{:S(2)}) copy-start(bf16[128,1024]{1,0:T(8,128)(2,1)} %get-tuple-element.8) | copy-start | bytes 786436
  55.7 8.3 %copy-start.1 = (bf16[128,1024]{0,1:T(8,128)(2,1)}, bf16[128,1024]{0,1:T(8,128)(2,1)S(1)}, u32[]{:S(2)}) copy-start(bf16[128,1024]{0,1:T(8,128)(2,1)S(1)} %copy.225) | copy-start | bytes 786436
  58.8 12.3 %all-to-all-start.1 = ((bf16[16,2,8,512]{3,0,1,2:T(8,128)(2,1)}), bf16[16,2,8,512]{3,0,1,2:T(8,128)(2,1)}, u32[]{:S(2)}, u32[]{:S(2)}) async-start(bf16[16,2,8,512]{3,0,1,2:T(8,128)(2,1)} %copy.185), calls=%async_computation.1 | async-start | bytes 524288 | tf_op jit(solution)/shard_map/all_to_all | solution.py:96
  62.8 0.7 copy-start.3
  71.1 1.3 copy-start.2
  72.4 1.0 copy-start.4
  74.8 1.0 copy-start
  80.0 0.8 copy-start.5
  82.2 6.9 %copy-start.6 = (bf16[8,128,2,128]{1,3,0,2:T(8,128)(2,1)S(1)}, bf16[8,128,2,128]{1,3,0,2:T(8,128)(2,1)}, u32[]{:S(2)}) copy-start(bf16[8,128,2,128]{1,3,0,2:T(8,128)(2,1)} %copy-done.5) | copy-start | bytes 1572868
  83.1 7.0 %copy-start.10 = (bf16[128,8,128]{2,0,1:T(8,128)(2,1)S(1)}, bf16[128,8,128]{2,0,1:T(8,128)(2,1)}, u32[]{:S(2)}) copy-start(bf16[128,8,128]{2,0,1:T(8,128)(2,1)} %fusion.28) | copy-start | bytes 786436
  85.0 12.3 %all-to-all-start.4 = ((bf16[16,2,8,512]{3,1,0,2:T(2,128)(2,1)}), bf16[16,2,8,512]{3,1,0,2:T(2,128)(2,1)}, u32[]{:S(2)}, u32[]{:S(2)}) async-start(bf16[16,2,8,512]{3,1,0,2:T(2,128)(2,1)} %copy.239), calls=%async_computation.4 | async-start | bytes 524288 | tf_op jit(solution)/shard_map/all_to_all | solution.py:111
  97.3 13.1 %all-to-all-start.6 = ((bf16[16,2,8,512]{3,1,0,2:T(2,128)(2,1)}), bf16[16,2,8,512]{3,1,0,2:T(2,128)(2,1)S(1)}, u32[]{:S(2)}, u32[]{:S(2)}) async-start(bf16[16,2,8,512]{3,1,0,2:T(2,128)(2,1)} %copy.247), calls=%async_computation.6 | async-start | bytes 524288 | tf_op jit(solution)/shard_map/all_to_all | solution.py:118
  102.3 22.8 %copy-start.7 = (bf16[128,1024]{1,0:T(8,128)(2,1)S(1)}, bf16[128,1024]{1,0:T(8,128)(2,1)}, u32[]{:S(2)}) copy-start(bf16[128,1024]{1,0:T(8,128)(2,1)} %copy.208) | copy-start | bytes 786436
  110.4 11.3 %all-to-all-start.5 = ((bf16[16,8,512]{2,0,1:T(8,128)(2,1)}), bf16[16,8,512]{2,0,1:T(8,128)(2,1)S(1)}, u32[]{:S(2)}, u32[]{:S(2)}) async-start(bf16[16,8,512]{2,0,1:T(8,128)(2,1)} %copy.241), calls=%async_computation.5 | async-start | bytes 262144 | tf_op jit(solution)/shard_map/all_to_all | solution.py:129
  121.8 10.7 %all-to-all-start.7 = ((bf16[16,8,512]{2,0,1:T(8,128)(2,1)}), bf16[16,8,512]{2,0,1:T(8,128)(2,1)S(1)}, u32[]{:S(2)}, u32[]{:S(2)}) async-start(bf16[16,8,512]{2,0,1:T(8,128)(2,1)} %copy.249), calls=%async_computation.7 | async-start | bytes 262144 | tf_op jit(solution)/shard_map/all_to_all | solution.py:130
where the time goes:
time: 135 us; the launch traced here: 134 us
  waiting for transfers between devices  36 us (27%)
  starting transfers between devices  33.8 us (25%)
  local copies, waits for them, and re-layouts  22.3 us (17%)
  blocking collectives  21.1 us (16%)
  matrix products  11.2 us (8%)
  other arithmetic  7.34 us (5%)
  between operations  1.9 us (1%)
    all_gather x1, blocking collectives, shards(): listed_all = lax.all_gather(block_lists, 'ctx', axis=0, tiled=True)  21.1 us
    all_to_all x1, starting transfers between devices, shards(): lax.all_to_all(episode_value_cache, 'ctx', split_axis=0, concat_axis=1, t...  7.28 us
    all_to_all x1, waiting for transfers between devices, shards(): lax.all_to_all(episode_key_cache, 'ctx', split_axis=0, concat_axis=1, til...  7.1 us
    all_to_all x1, waiting for transfers between devices, shards(): lax.all_to_all(picked_values, 'ctx', split_axis=2, concat_axis=2, tiled=T...  6.83 us
    all_to_all x1, waiting for transfers between devices, shards(): lax.all_to_all(row_key_grad, 'ctx', split_axis=1, concat_axis=0, tiled=True)  6.53 us
    unnamed x37, local copies, waits for them, and re-layouts  6.16 us
    all_to_all x1, waiting for transfers between devices, shards(): lax.all_to_all(split_rows(value_pieces, row_count).astype(jnp.bfloat16),...  6.15 us
    all_to_all x1, waiting for transfers between devices, shards(): lax.all_to_all(row_value_grad, 'ctx', split_axis=1, concat_axis=0, tiled=...  5.78 us
  transfers between devices with their start and end apart: 8, of which 7 were waited for; matrix products, arithmetic and copies ran while one was open for 15% of the time, Pallas kernels for 0%

commit v1 on v0

--- a/solution.py
+++ b/solution.py
@@ -1,3 +1,4 @@
+import functools
 import jax
 import jax.numpy as jnp
 from jax import lax
@@ -7,6 +8,18 @@
 KEY_VALUE_HEADS = 8
 HEAD_SIZE = 128
 LIST = 2
+
+
+def remake_layers_all(buf, axis_name):
+    main = lax.axis_size(axis_name)
+    mid_arr = jnp.split(buf, main, 0)
+    f_next = jnp.stack(mid_arr)
+    odd = lax.all_to_all(f_next, axis_name, 0, 0)
+    long_array = jnp.concatenate(odd, 1)
+    return long_array
+
+
+part_values_for = functools.partial(remake_layers_all, axis_name="ctx")
 
 
 def attend_group(query_part, key_part, value_part, grad_part, live_slots):
@@ -63,7 +76,7 @@
     queries, episode_key_cache, episode_value_cache, output_gradient, block_lists, block_counts
 ):
     held_keys, held_values = (
-        lax.all_to_all(episode_key_cache, "ctx", split_axis=0, concat_axis=1, tiled=True),
+        part_values_for(episode_key_cache),
         lax.all_to_all(episode_value_cache, "ctx", split_axis=0, concat_axis=1, tiled=True),
     )
     row_count = held_keys.shape[0]

time: 135 us -> 143 us (1.059)
  local copies, waits for them, and re-layouts: 22.3 us -> 32 us
  other arithmetic: 7.34 us -> 5.75 us
    unnamed x37 -> x41, local copies, waits for them, and re-layouts: 6.16 us -> 14.5 us
    unnamed x2 -> x1, other arithmetic: 3.16 us -> 1.58 us
  transfers between devices with their start and end apart: 8 -> 8, of which waited for: 7 -> 7; matrix products, arithmetic and copies ran while one was open for 15% -> 20% of each run, Pallas kernels for 0% -> 0%
where the time goes in v1:
time: 143 us; the launch traced here: 141 us
  waiting for transfers between devices  35.5 us (25%)
  starting transfers between devices  33.8 us (24%)
  local copies, waits for them, and re-layouts  32 us (22%)
  blocking collectives  21.1 us (15%)
  matrix products  11.2 us (8%)
  other arithmetic  5.75 us (4%)
  between operations  1.89 us (1%)
    all_gather x1, blocking collectives, shards(): listed_all = lax.all_gather(block_lists, 'ctx', axis=0, tiled=True)  21.1 us
    unnamed x41, local copies, waits for them, and re-layouts  14.5 us
    all_to_all x1, starting transfers between devices, shards(): lax.all_to_all(episode_value_cache, 'ctx', split_axis=0, concat_axis=1, t...  7.28 us
    all_to_all x1, waiting for transfers between devices, shards(): lax.all_to_all(picked_values, 'ctx', split_axis=2, concat_axis=2, tiled=T...  6.83 us
    all_to_all x1, waiting for transfers between devices, shards(): lax.all_to_all(row_key_grad, 'ctx', split_axis=1, concat_axis=0, tiled=True)  6.53 us
    all_to_all x1, waiting for transfers between devices, remake_layers_all(): odd = lax.all_to_all(f_next, axis_name, 0, 0)  6.52 us
    all_to_all x1, waiting for transfers between devices, shards(): lax.all_to_all(split_rows(value_pieces, row_count).astype(jnp.bfloat16),...  6.15 us
    all_to_all x1, waiting for transfers between devices, shards(): lax.all_to_all(row_value_grad, 'ctx', split_axis=1, concat_axis=0, tiled=...  5.78 us
  transfers between devices with their start and end apart: 8, of which 7 were waited for; matrix products, arithmetic and copies ran while one was open for 20% of the time, Pallas kernels for 0%

profile of v1, /device:TPU:0, one launch (start us, length us, event | category | flops | bytes accessed | tf_op | source)
XLA Modules:
  0.0 141.3 jit_solution(12382182508718753458)
XLA Ops:
  1.1 1.6 %reduce = bf16[128,512]{1,0:T(8,128)(2,1)S(1)} reduce(bf16[128,1,512]{2,0,1:T(8,128)(2,1)} %param.10, bf16[]{:T(256)} %broadcast.110), dimensions={1}, to_apply=%copy.183.reduce_sub_computation | reduce | bytes 262146 | tf_op args[2]
  3.5 7.3 %all-to-all-start = ((bf16[8,2,4096]{2,1,0:T(2,128)(2,1)}), bf16[8,2,4096]{2,1,0:T(2,128)(2,1)S(1)}, u32[]{:S(2)}, u32[]{:S(2)}) async-start(bf16[8,2,4096]{2,1,0:T(2,128)(2,1)} %reshape.195), calls=%async_computation | async-start | bytes 262144 | tf_op jit(solution)/shard_map/all_to_all | solution.py:80
  10.7 21.1 %all-gather = s32[8,1,2]{2,1,0:T(1,128)S(1)} all-gather(s32[1,1,2]{2,1,0:T(1,128)} %bitcast.481), channel_id=1, replica_groups=mesh['parts'=2,'ctx'=8,'tp'=2] {'ctx'}, dimensions={0}, use_global_device_ids=true | all-gather | bytes 72 | tf_op jit(solution)/shard_map/all_gather | solution.py:87
  32.0 1.3 constant_dynamic-update-slice_fusion.7
  33.3 1.3 constant_dynamic-update-slice_fusion.6
  34.6 1.3 constant_dynamic-update-slice_fusion.5
  35.9 1.3 constant_dynamic-update-slice_fusion.4
  37.3 1.3 constant_dynamic-update-slice_fusion.3
  38.6 1.3 constant_dynamic-update-slice_fusion.2
  39.9 1.3 constant_dynamic-update-slice_fusion.1
  41.3 1.3 constant_dynamic-update-slice_fusion
  42.6 3.4 %all-to-all-start.2 = ((bf16[8,16,1,512]{3,1,2,0:T(8,128)(2,1)}), bf16[8,16,1,512]{3,1,2,0:T(8,128)(2,1)S(1)}, u32[]{:S(2)}, u32[]{:S(2)}) async-start(bf16[8,16,1,512]{3,1,2,0:T(8,128)(2,1)} %constant_dynamic-update-slice_fusion), calls=%async_computation.2 | async-start | bytes 262144 | tf_op jit(solution)/shard_map/all_to_all | solution.py:17
  46.8 6.5 %all-to-all-done.2 = bf16[8,16,1,512]{3,1,2,0:T(8,128)(2,1)S(1)} async-done(((bf16[8,16,1,512]{3,1,2,0:T(8,128)(2,1)}), bf16[8,16,1,512]{3,1,2,0:T(8,128)(2,1)S(1)}, u32[]{:S(2)}, u32[]{:S(2)}) %all-to-all-start.2) | async-done | bytes 131104 | tf_op jit(solution)/shard_map/all_to_all | solution.py:17
  54.7 3.4 %all-to-all-start.3 = ((bf16[16,2,8,512]{3,0,1,2:T(8,128)(2,1)}), bf16[16,2,8,512]{3,0,1,2:T(8,128)(2,1)S(1)}, u32[]{:S(2)}, u32[]{:S(2)}) async-start(bf16[16,2,8,512]{3,0,1,2:T(8,128)(2,1)} %copy.187), calls=%async_computation.3 | async-start | bytes 524288 | tf_op jit(solution)/shard_map/all_to_all | solution.py:108
  61.0 1.2 copy.208
  64.1 2.2 %all-to-all-done.3 = bf16[16,2,8,512]{3,0,1,2:T(8,128)(2,1)S(1)} async-done(((bf16[16,2,8,512]{3,0,1,2:T(8,128)(2,1)}), bf16[16,2,8,512]{3,0,1,2:T(8,128)(2,1)S(1)}, u32[]{:S(2)}, u32[]{:S(2)}) %all-to-all-start.3) | async-done | bytes 262176 | tf_op jit(solution)/shard_map/all_to_all | solution.py:108
  66.3 4.0 %all-to-all-start.1 = ((bf16[16,2,8,512]{3,0,1,2:T(8,128)(2,1)}), bf16[16,2,8,512]{3,0,1,2:T(8,128)(2,1)}, u32[]{:S(2)}, u32[]{:S(2)}) async-start(bf16[16,2,8,512]{3,0,1,2:T(8,128)(2,1)} %copy.184), calls=%async_computation.1 | async-start | bytes 524288 | tf_op jit(solution)/shard_map/all_to_all | solution.py:109
  71.8 6.8 %all-to-all-done.1 = bf16[16,2,8,512]{3,0,1,2:T(8,128)(2,1)} async-done(((bf16[16,2,8,512]{3,0,1,2:T(8,128)(2,1)}), bf16[16,2,8,512]{3,0,1,2:T(8,128)(2,1)}, u32[]{:S(2)}, u32[]{:S(2)}) %all-to-all-start.1) | async-done | bytes 262176 | tf_op jit(solution)/shard_map/all_to_all | solution.py:109
  78.6 1.0 copy.185
  90.6 2.0 %copy.237 = bf16[16,2,8,512]{3,1,0,2:T(2,128)(2,1)} copy(bf16[16,2,8,512]{3,0,2,1:T(8,128)(2,1)} %bitcast.461) | data formatting | bytes 524288 | tf_op jit(solution)/shard_map/convert_element_type | solution.py:125
  92.6 4.0 %all-to-all-start.4 = ((bf16[16,2,8,512]{3,1,0,2:T(2,128)(2,1)}), bf16[16,2,8,512]{3,1,0,2:T(2,128)(2,1)}, u32[]{:S(2)}, u32[]{:S(2)}) async-start(bf16[16,2,8,512]{3,1,0,2:T(2,128)(2,1)} %copy.237), calls=%async_computation.4 | async-start | bytes 524288 | tf_op jit(solution)/shard_map/all_to_all | solution.py:124
  97.9 1.1 copy.229
  99.1 1.1 copy.230
  103.4 1.5 %all-to-all-done.4 = bf16[16,2,8,512]{3,1,0,2:T(2,128)(2,1)} async-done(((bf16[16,2,8,512]{3,1,0,2:T(2,128)(2,1)}), bf16[16,2,8,512]{3,1,0,2:T(2,128)(2,1)}, u32[]{:S(2)}, u32[]{:S(2)}) %all-to-all-start.4) | async-done | bytes 262176 | tf_op jit(solution)/shard_map/all_to_all | solution.py:124
  104.9 4.4 %all-to-all-start.6 = ((bf16[16,2,8,512]{3,1,0,2:T(2,128)(2,1)}), bf16[16,2,8,512]{3,1,0,2:T(2,128)(2,1)S(1)}, u32[]{:S(2)}, u32[]{:S(2)}) async-start(bf16[16,2,8,512]{3,1,0,2:T(2,128)(2,1)} %copy.245), calls=%async_computation.6 | async-start | bytes 524288 | tf_op jit(solution)/shard_map/all_to_all | solution.py:131
  109.9 1.2 fusion.39
  111.8 6.1 %all-to-all-done.6 = bf16[16,2,8,512]{3,1,0,2:T(2,128)(2,1)S(1)} async-done(((bf16[16,2,8,512]{3,1,0,2:T(2,128)(2,1)}), bf16[16,2,8,512]{3,1,0,2:T(2,128)(2,1)S(1)}, u32[]{:S(2)}, u32[]{:S(2)}) %all-to-all-start.6) | async-done | bytes 262176 | tf_op jit(solution)/shard_map/all_to_all | solution.py:131
  118.0 3.8 %all-to-all-start.5 = ((bf16[16,8,512]{2,0,1:T(8,128)(2,1)}), bf16[16,8,512]{2,0,1:T(8,128)(2,1)S(1)}, u32[]{:S(2)}, u32[]{:S(2)}) async-start(bf16[16,8,512]{2,0,1:T(8,128)(2,1)} %copy.239), calls=%async_computation.5 | async-start | bytes 262144 | tf_op jit(solution)/shard_map/all_to_all | solution.py:142
  122.8 6.5 %all-to-all-done.5 = bf16[16,8,512]{2,0,1:T(8,128)(2,1)S(1)} async-done(((bf16[16,8,512]{2,0,1:T(8,128)(2,1)}), bf16[16,8,512]{2,0,1:T(8,128)(2,1)S(1)}, u32[]{:S(2)}, u32[]{:S(2)}) %all-to-all-start.5) | async-done | bytes 131104 | tf_op jit(solution)/shard_map/all_to_all | solution.py:142
  129.3 3.4 %all-to-all-start.7 = ((bf16[16,8,512]{2,0,1:T(8,128)(2,1)}), bf16[16,8,512]{2,0,1:T(8,128)(2,1)S(1)}, u32[]{:S(2)}, u32[]{:S(2)}) async-start(bf16[16,8,512]{2,0,1:T(8,128)(2,1)} %copy.247), calls=%async_computation.7 | async-start | bytes 262144 | tf_op jit(solution)/shard_map/all_to_all | solution.py:143
  132.7 1.5 %pad_maximum_fusion = (bf16[128,4096]{1,0:T(8,128)(2,1)}, bf16[128,4096]{1,0:T(8,128)(2,1)}) fusion(bf16[128,1024]{1,0:T(8,128)(2,1)S(1)} %copy.207, bf16[128,1024]{1,0:T(8,128)(2,1)S(1)} %copy-done.7, bf16[128,1024]{1,0:T(8,128)(2,1)S(1)} %copy.205, bf16[128,1024]{1,0:T(8,128)(2,1)S(1)} %copy.204, bf16[128,1024]{1,0:T(8,128)(2,1)S(1)} %copy.231, ...), kind=kLoop, calls=%fused_computation.80 | loop fusion | flops 8388608 | bytes 4194304 | tf_op jit(solution)/shard_map/concatenate | solution.py:145
  134.2 5.8 %all-to-all-done.7 = bf16[16,8,512]{2,0,1:T(8,128)(2,1)S(1)} async-done(((bf16[16,8,512]{2,0,1:T(8,128)(2,1)}), bf16[16,8,512]{2,0,1:T(8,128)(2,1)S(1)}, u32[]{:S(2)}, u32[]{:S(2)}) %all-to-all-start.7) | async-done | bytes 131104 | tf_op jit(solution)/shard_map/all_to_all | solution.py:143
  (102 shorter events, 27.8 us)
Async XLA Ops:
  3.5 39.2 %all-to-all-start = ((bf16[8,2,4096]{2,1,0:T(2,128)(2,1)}), bf16[8,2,4096]{2,1,0:T(2,128)(2,1)S(1)}, u32[]{:S(2)}, u32[]{:S(2)}) async-start(bf16[8,2,4096]{2,1,0:T(2,128)(2,1)} %reshape.195), calls=%async_computation | async-start | bytes 262144 | tf_op jit(solution)/shard_map/all_to_all | solution.py:80
  42.6 10.7 %all-to-all-start.2 = ((bf16[8,16,1,512]{3,1,2,0:T(8,128)(2,1)}), bf16[8,16,1,512]{3,1,2,0:T(8,128)(2,1)S(1)}, u32[]{:S(2)}, u32[]{:S(2)}) async-start(bf16[8,16,1,512]{3,1,2,0:T(8,128)(2,1)} %constant_dynamic-update-slice_fusion), calls=%async_computation.2 | async-start | bytes 262144 | tf_op jit(solution)/shard_map/all_to_all | solution.py:17
  53.9 4.3 %copy-start.8 = (bf16[128,4096]{1,0:T(8,128)(2,1)S(1)}, bf16[128,4096]{1,0:T(8,128)(2,1)}, u32[]{:S(2)}) copy-start(bf16[128,4096]{1,0:T(8,128)(2,1)} %param.8) | copy-start | bytes 3145732
  54.7 11.6 %all-to-all-start.3 = ((bf16[16,2,8,512]{3,0,1,2:T(8,128)(2,1)}), bf16[16,2,8,512]{3,0,1,2:T(8,128)(2,1)S(1)}, u32[]{:S(2)}, u32[]{:S(2)}) async-start(bf16[16,2,8,512]{3,0,1,2:T(8,128)(2,1)} %copy.187), calls=%async_computation.3 | async-start | bytes 524288 | tf_op jit(solution)/shard_map/all_to_all | solution.py:108
  58.9 1.2 copy-start.9
  61.0 2.2 %copy-start.11 = (bf16[128,1024]{1,0:T(8,128)(2,1)S(1)}, bf16[128,1024]{1,0:T(8,128)(2,1)}, u32[]{:S(2)}) copy-start(bf16[128,1024]{1,0:T(8,128)(2,1)} %get-tuple-element.8) | copy-start | bytes 786436
  63.2 8.3 %copy-start.1 = (bf16[128,1024]{0,1:T(8,128)(2,1)}, bf16[128,1024]{0,1:T(8,128)(2,1)S(1)}, u32[]{:S(2)}) copy-start(bf16[128,1024]{0,1:T(8,128)(2,1)S(1)} %copy.223) | copy-start | bytes 786436
  66.3 12.3 %all-to-all-start.1 = ((bf16[16,2,8,512]{3,0,1,2:T(8,128)(2,1)}), bf16[16,2,8,512]{3,0,1,2:T(8,128)(2,1)}, u32[]{:S(2)}, u32[]{:S(2)}) async-start(bf16[16,2,8,512]{3,0,1,2:T(8,128)(2,1)} %copy.184), calls=%async_computation.1 | async-start | bytes 524288 | tf_op jit(solution)/shard_map/all_to_all | solution.py:109
  70.4 0.7 copy-start.3
  78.6 1.3 copy-start.2
  80.0 1.0 copy-start.4
  82.3 1.0 copy-start
  87.6 0.8 copy-start.5
  89.7 6.9 %copy-start.6 = (bf16[8,128,2,128]{1,3,0,2:T(8,128)(2,1)S(1)}, bf16[8,128,2,128]{1,3,0,2:T(8,128)(2,1)}, u32[]{:S(2)}) copy-start(bf16[8,128,2,128]{1,3,0,2:T(8,128)(2,1)} %copy-done.5) | copy-start | bytes 1572868
  90.6 7.0 %copy-start.10 = (bf16[128,8,128]{2,0,1:T(8,128)(2,1)S(1)}, bf16[128,8,128]{2,0,1:T(8,128)(2,1)}, u32[]{:S(2)}) copy-start(bf16[128,8,128]{2,0,1:T(8,128)(2,1)} %fusion.28) | copy-start | bytes 786436
  92.6 12.3 %all-to-all-start.4 = ((bf16[16,2,8,512]{3,1,0,2:T(2,128)(2,1)}), bf16[16,2,8,512]{3,1,0,2:T(2,128)(2,1)}, u32[]{:S(2)}, u32[]{:S(2)}) async-start(bf16[16,2,8,512]{3,1,0,2:T(2,128)(2,1)} %copy.237), calls=%async_computation.4 | async-start | bytes 524288 | tf_op jit(solution)/shard_map/all_to_all | solution.py:124
  104.9 13.1 %all-to-all-start.6 = ((bf16[16,2,8,512]{3,1,0,2:T(2,128)(2,1)}), bf16[16,2,8,512]{3,1,0,2:T(2,128)(2,1)S(1)}, u32[]{:S(2)}, u32[]{:S(2)}) async-start(bf16[16,2,8,512]{3,1,0,2:T(2,128)(2,1)} %copy.245), calls=%async_computation.6 | async-start | bytes 524288 | tf_op jit(solution)/shard_map/all_to_all | solution.py:131
  109.9 22.8 %copy-start.7 = (bf16[128,1024]{1,0:T(8,128)(2,1)S(1)}, bf16[128,1024]{1,0:T(8,128)(2,1)}, u32[]{:S(2)}) copy-start(bf16[128,1024]{1,0:T(8,128)(2,1)} %copy.206) | copy-start | bytes 786436
  118.0 11.3 %all-to-all-start.5 = ((bf16[16,8,512]{2,0,1:T(8,128)(2,1)}), bf16[16,8,512]{2,0,1:T(8,128)(2,1)S(1)}, u32[]{:S(2)}, u32[]{:S(2)}) async-start(bf16[16,8,512]{2,0,1:T(8,128)(2,1)} %copy.239), calls=%async_computation.5 | async-start | bytes 262144 | tf_op jit(solution)/shard_map/all_to_all | solution.py:142
  129.3 10.7 %all-to-all-start.7 = ((bf16[16,8,512]{2,0,1:T(8,128)(2,1)}), bf16[16,8,512]{2,0,1:T(8,128)(2,1)S(1)}, u32[]{:S(2)}, u32[]{:S(2)}) async-start(bf16[16,8,512]{2,0,1:T(8,128)(2,1)} %copy.247), calls=%async_computation.7 | async-start | bytes 262144 | tf_op jit(solution)/shard_map/all_to_all | solution.py:143
